TPU v7x, 32 devices: a whole 2x2x4 slice. The times are simulated.
32 devices in a mesh: ctx: 4 (over y, x), tp: 8 (over z, core).
Axes of the slice: x: 2, y: 2, z: 4, core: 2. Of those that a mesh axis runs over, the one named last changes fastest.
Arguments:
- resid: bfloat16 [1024, 4096], P('ctx', 'tp'), may hold values from -6 to 6
- attn_gain: bfloat16 [4096], replicated, may hold values from 0.5 to 1.5
- mlp_gain: bfloat16 [4096], replicated, may hold values from 0.5 to 1.5
- w_query: bfloat16 [4096, 4096], P(None, 'tp'), may hold values from -0.09375 to 0.09375
- w_kv: bfloat16 [4096, 1024], P(None, 'tp'), may hold values from -0.09375 to 0.09375
- w_out: bfloat16 [4096, 4096], P('tp'), may hold values from -0.09375 to 0.09375
- w_gate: bfloat16 [4096, 11008], P(None, 'tp'), may hold values from -0.09375 to 0.09375
- w_up: bfloat16 [4096, 11008], P(None, 'tp'), may hold values from -0.09375 to 0.09375
- w_down: bfloat16 [11008, 4096], P('tp'), may hold values from -0.0546875 to 0.0546875
- kv_cache: bfloat16 [32, 128, 1024], P('ctx'), may hold values from -70 to 70
- cache_len: int32 [4], replicated, may hold values from 1 to 2048
- span_len: int32 [4], replicated, may hold values from 1 to 256
- slot_req: int32 [32], P('ctx'), may hold values from 0 to 4, as said below
- slot_blk: int32 [32], P('ctx'), may hold values from 0 to 15, as said below
Outputs:
- layer_out: bfloat16 [1024, 4096], P('ctx', 'tp')
- new_kv: bfloat16 [1024, 1024], P('ctx', 'tp')
Inputs may be any that keep to these rules, and one draw needn't show every extreme that they name: `slot_req`: each request r holds ceil(cache_len[r] / 128) blocks, and each of its blocks stands in exactly one slot; every other slot is empty. `slot_blk`: block numbers of live slots are below their request's block count; empty slots carry 0.
All inputs are finite; a program needn't handle non-finite values.
Results may differ from a plain program's by a relative error of at most 0.035.
Values may be sent and summed in bfloat16 or wider, within the bound.
No kernel may reach another device: no remote copies, remote signals or barrier semaphores. Data moves between devices by JAX's collectives and lax.ppermute only.
A program may use at most 128 MiB of HBM per device.

v0:
```python
import jax
import jax.numpy as jnp
from jax import lax
from jax.sharding import PartitionSpec as P

HQ = 32
KVH = 4
HD = 128
BLK = 128
THETA = 5000000.0
EPS = 1e-05
NEG = -1e30


def rms_norm(values, gain):
    wide = values.astype(jnp.float32)
    factor = lax.rsqrt(jnp.mean(wide * wide, axis=-1, keepdims=True) + EPS)
    return (wide * factor * gain.astype(jnp.float32)).astype(jnp.bfloat16)


def rotate(vectors, positions):
    width = vectors.shape[-1]
    half = width // 2
    freqs = THETA ** (-(jnp.arange(half, dtype=jnp.float32) * 2.0 / width))
    angles = positions.astype(jnp.float32)[:, None] * freqs[None, :]
    cosine = jnp.cos(angles)[:, None, :]
    sine = jnp.sin(angles)[:, None, :]
    first = vectors[..., :half]
    second = vectors[..., half:]
    return jnp.concatenate(
        [first * cosine - second * sine, second * cosine + first * sine], axis=-1
    )


def column_term(rows, weight):
    return lax.dot_general(
        weight, rows, (((0,), (1,)), ((), ())), preferred_element_type=jnp.float32
    )


def gather_ctx(value, count):
    parts = [value]
    for shift in range(1, count):
        pairs = [(i, (i + shift) % count) for i in range(count)]
        parts.append(lax.ppermute(value, "ctx", pairs))
    return parts


def per_device(
    resid,
    attn_gain,
    mlp_gain,
    w_query,
    w_kv,
    w_out,
    w_gate,
    w_up,
    w_down,
    kv_cache,
    cache_len,
    span_len,
    slot_req,
    slot_blk,
):
    span_size = resid.shape[0]
    ctx_count = lax.axis_size("ctx")
    q_cols = w_query.shape[1]
    heads_dev = q_cols // HD
    ctx_rank = lax.axis_index("ctx")
    tp_rank = lax.axis_index("tp")
    group = tp_rank * heads_dev // (HQ // KVH)
    my_len = cache_len[ctx_rank]
    my_span = span_len[ctx_rank]
    offsets = jnp.arange(span_size, dtype=jnp.int32)
    positions = my_len + offsets
    live_rows = offsets < my_span
    own_cache = jnp.concatenate(
        [
            lax.dynamic_slice_in_dim(kv_cache, group * HD, HD, 2),
            lax.dynamic_slice_in_dim(kv_cache, KVH * HD + group * HD, HD, 2),
        ],
        axis=2,
    )
    own_meta = jnp.stack([slot_req, slot_blk])
    cache_all = jnp.concatenate(gather_ctx(own_cache, ctx_count), axis=0)
    meta_all = jnp.concatenate(gather_ctx(own_meta, ctx_count), axis=1)
    full_resid = lax.all_gather(resid, "tp", axis=1, tiled=True)
    x_norm = rms_norm(full_resid, attn_gain)
    query = rotate(
        jnp.dot(x_norm, w_query, preferred_element_type=jnp.float32).reshape(
            span_size, heads_dev, HD
        ),
        positions,
    ).astype(jnp.bfloat16)
    kv_piece = jnp.dot(x_norm, w_kv, preferred_element_type=jnp.float32).astype(jnp.bfloat16)
    kv_width = kv_piece.shape[1]
    kv_all = lax.all_gather(kv_piece, "tp", axis=1, tiled=True)
    all_keys = rotate(
        kv_all[:, : KVH * HD].astype(jnp.float32).reshape(span_size, KVH, HD), positions
    ).astype(jnp.bfloat16)
    joined = jnp.concatenate([all_keys.reshape(span_size, KVH * HD), kv_all[:, KVH * HD :]], axis=1)
    mine = lax.dynamic_slice_in_dim(joined, tp_rank * kv_width, kv_width, 1)
    new_kv = jnp.where(live_rows[:, None], mine, jnp.zeros_like(mine))
    new_keys = lax.dynamic_index_in_dim(all_keys, group, 1, keepdims=False)
    new_vals = lax.dynamic_slice_in_dim(kv_all, KVH * HD + group * HD, HD, 1)
    cache_rows = cache_all.shape[0] * BLK
    keys = jnp.concatenate([cache_all[..., :HD].reshape(cache_rows, HD), new_keys], axis=0)
    vals = jnp.concatenate([cache_all[..., HD:].reshape(cache_rows, HD), new_vals], axis=0)
    key_pos = meta_all[1][:, None] * BLK + jnp.arange(BLK, dtype=jnp.int32)[None, :]
    cache_ok = ((meta_all[0][:, None] == ctx_rank) & (key_pos < my_len)).reshape(cache_rows)
    new_ok = (offsets[None, :] <= offsets[:, None]) & (offsets[None, :] < my_span)
    valid = jnp.concatenate(
        [jnp.broadcast_to(cache_ok[None, :], (span_size, cache_rows)), new_ok], axis=1
    )
    scores = jnp.einsum("chd,kd->hck", query, keys, preferred_element_type=jnp.float32) * HD ** (
        -0.5
    )
    peak = jnp.max(jnp.where(valid[None], scores, NEG), axis=2)
    weights = jnp.where(valid[None], jnp.exp(scores - peak[..., None]), 0.0)
    total = jnp.sum(weights, axis=2)
    summed = jnp.einsum(
        "hck,kd->hcd", weights.astype(jnp.bfloat16), vals, preferred_element_type=jnp.float32
    )
    attn_rows = (
        (summed / total[..., None])
        .transpose(1, 0, 2)
        .reshape(span_size, q_cols)
        .astype(jnp.bfloat16)
    )
    head_sum = lax.psum_scatter(
        column_term(attn_rows, w_out).astype(jnp.bfloat16), "tp", scatter_dimension=0, tiled=True
    ).astype(jnp.float32)
    mid = (resid.astype(jnp.float32) + head_sum.T).astype(jnp.bfloat16)
    full_mid = lax.all_gather(mid, "tp", axis=1, tiled=True)
    x_two = rms_norm(full_mid, mlp_gain)
    gate = jnp.dot(x_two, w_gate, preferred_element_type=jnp.float32)
    up_part = jnp.dot(x_two, w_up, preferred_element_type=jnp.float32)
    hidden = (jax.nn.silu(gate) * up_part).astype(jnp.bfloat16)
    down_sum = lax.psum_scatter(
        column_term(hidden, w_down).astype(jnp.bfloat16), "tp", scatter_dimension=0, tiled=True
    ).astype(jnp.float32)
    layer_out = (mid.astype(jnp.float32) + down_sum.T).astype(jnp.bfloat16)
    layer_out = jnp.where(live_rows[:, None], layer_out, jnp.zeros_like(layer_out))
    return (layer_out, new_kv)


def solution(mesh):
    return jax.shard_map(
        per_device,
        mesh=mesh,
        in_specs=(
            P("ctx", "tp"),
            P(),
            P(),
            P(None, "tp"),
            P(None, "tp"),
            P("tp", None),
            P(None, "tp"),
            P(None, "tp"),
            P("tp", None),
            P("ctx", None, None),
            P(),
            P(),
            P("ctx"),
            P("ctx"),
        ),
        out_specs=(P("ctx", "tp"), P("ctx", "tp")),
        check_vma=False,
    )
```

profile of v0, /device:TPU:0, one launch (start us, length us, event | category | flops | bytes accessed | tf_op | source)
XLA Modules:
  0.0 242.1 jit_solution(6783432989193067769)
XLA Ops:
  8.6 3.9 %collective-permute-start.2 = (s32[2,8]{1,0:T(2,128)S(1)}, s32[2,8]{1,0:T(2,128)S(1)}, u32[]{:S(2)}, u32[]{:S(2)}) collective-permute-start(s32[2,8]{1,0:T(2,128)S(1)} %pad_add_fusion.1), channel_id=1, source_target_pairs={{0,24},{8,0},{16,8},{24,16},{1,25},{9,1},{17,9},{25,17},{2,26},{10... | collective-permute-start | bytes 200 | tf_op jit(solution)/shard_map/ppermute | solution.py:45
  14.8 2.4 collective-permute-start.5
  17.2 1.5 collective-permute-start.4
  18.7 1.2 dynamic_slice.22
  19.9 1.3 dynamic_slice.23
  25.5 5.1 %pad_add_fusion = pred[256,4352]{0,1:T(8,128)(4,1)} fusion(pred[256,256]{0,1:T(8,128)(4,1)S(1)} %fusion.46, pred[4352]{0:T(1024)(128)(4,1)S(1)} %pad.8.clone), kind=kLoop, calls=%fused_computation.20 | loop fusion | flops 1114112 | bytes 1184000 | tf_op jit(solution)/shard_map/concatenate | solution.py:112
  30.6 10.4 %collective-permute-done.4 = bf16[8,128,256]{2,1,0:T(8,128)(2,1)S(1)} collective-permute-done((bf16[8,128,256]{2,1,0:T(8,128)(2,1)S(1)}, bf16[8,128,256]{2,1,0:T(8,128)(2,1)S(1)}, u32[]{:S(2)}, u32[]{:S(2)}) %collective-permute-start.4) | collective-permute-done | bytes 524320 | tf_op jit(solution)/shard_map/ppermute | solution.py:45
  41.8 1.3 copy.25
  43.1 2.2 fusion.12
  45.4 2.6 %convolution_convert_fusion.2 = bf16[256,128]{1,0:T(8,128)(2,1)S(1)} fusion(bf16[4096,128]{1,0:T(8,128)(2,1)S(1)} %copy-done, bf16[256,4096]{1,0:T(8,128)(2,1)} %all-gather.3.cloned.1.call-done, f32[4096]{0:T(1024)S(1)} %convert_element_type.78, f32[256]{0:T(256)S(1)} %add_rsqrt_fusion.1), kind=kOutput, calls=%fused_computation.33 | convolution fusion | flops 272662528 | bytes 3228672 | tf_op jit(solution)/shard_map/dot_general | solution.py:95
  48.0 14.3 %all_gather.10 = bf16[256,1024]{1,0:T(8,128)(2,1)S(1)} all-gather(bf16[256,128]{1,0:T(8,128)(2,1)S(1)} %convolution_convert_fusion.2), channel_id=1, replica_groups=mesh['ctx'=4,'tp'=8] {'tp'}, dimensions={1}, use_global_device_ids=true | all-gather | bytes 589824 | tf_op jit(solution)/shard_map/all_gather | solution.py:97
  62.4 1.3 fusion.37
  65.3 8.7 %fusion.30 = f32[4352,256,4]{1,0,2:T(8,128)} fusion(bf16[256,128]{1,0:T(8,128)(2,1)S(1)} %dynamic-slice_bitcast_fusion, bf16[4096,128]{1,0:T(8,128)(2,1)S(1)} %bitcast.69, bf16[256,4,64]{2,0,1:T(8,128)(2,1)S(1)} %get-tuple-element.7, bf16[256,4,64]{2,0,1:T(8,128)(2,1)S(1)} %get-tuple-element.6), kind=kOutput, calls=%fused_computation.38 | convolution fusion | flops 1143603200 | bytes 19202048 | tf_op jit(solution)/shard_map/chd,kd->hck/dot_general | solution.py:115
  74.0 18.6 %fusion.60 = (f32[4,256]{1,0:T(4,128)S(1)}, bf16[4,256,4352]{1,2,0:T(8,128)(2,1)}) fusion(f32[4352,256,4]{1,0,2:T(8,128)} %fusion.30, pred[256,4352]{0,1:T(8,128)(4,1)} %pad_add_fusion), kind=kOutput, calls=%fused_computation.92 | output fusion | flops 31199488 | bytes 27856896 | tf_op jit(solution)/shard_map/sub | solution.py:119
  92.6 5.0 %fusion.25 = bf16[256,4,128]{0,2,1:T(8,128)(2,1)S(1)} fusion(bf16[4,256,4352]{1,2,0:T(8,128)(2,1)} %get-tuple-element.19, bf16[256,128]{0,1:T(8,128)(2,1)S(1)} %copy.21, bf16[4096,128]{0,1:T(8,128)(2,1)S(1)} %copy-done.6, f32[256,4]{0,1:T(4,128)S(1)} %bitcast.76), kind=kOutput, calls=%fused_computation.32 | convolution fusion | flops 1143341056 | bytes 10293248 | tf_op jit(solution)/shard_map/hck,kd->hcd/dot_general | solution.py:121
  97.7 2.7 %fusion.11 = bf16[4096,256]{0,1:T(8,128)(2,1)} fusion(bf16[256,512]{0,1:T(8,128)(2,1)S(1)} %bitcast.71, bf16[512,4096]{1,0:T(8,128)(2,1)S(1)} %copy-done.2), kind=kOutput, calls=%fused_computation.19 | convolution fusion | flops 1074790400 | bytes 6553600 | tf_op jit(solution)/shard_map/dot_general | solution.py:36
  100.4 34.6 %reduce-scatter.3.cloned.1.call-done = bf16[512,256]{0,1:T(8,128)(2,1)} async-done(((bf16[4096,256]{0,1:T(8,128)(2,1)}), bf16[512,256]{0,1:T(8,128)(2,1)}) %reduce-scatter.3.cloned.1.call-update) | async-done | bytes 262160 | tf_op jit(solution)/shard_map/reduce_scatter | solution.py:130
  135.0 1.7 fusion.41
  137.1 27.9 %all-gather.5.cloned.1.call-done = bf16[256,4096]{1,0:T(8,128)(2,1)} async-done(((bf16[256,512]{1,0:T(8,128)(2,1)}), bf16[256,4096]{1,0:T(8,128)(2,1)}) %all-gather.5.cloned.1.call-update) | async-done | bytes 2097168 | tf_op jit(solution)/shard_map/all_gather | solution.py:134
  164.9 2.1 fusion.15
  167.0 9.2 %fusion.35 = f32[256,1376]{0,1:T(8,128)} fusion(bf16[4096,1376]{0,1:T(8,128)(2,1)} %param.20, bf16[256,4096]{1,0:T(8,128)(2,1)} %all-gather.5.cloned.1.call-done, f32[4096]{0:T(1024)S(1)} %convert_element_type.91, f32[256]{0:T(256)S(1)} %add_rsqrt_fusion), kind=kOutput, calls=%fused_computation.41 | convolution fusion | flops 2889875456 | bytes 14795776 | tf_op jit(solution)/shard_map/dot_general | solution.py:136
  176.2 22.1 %fusion.10 = bf16[4096,256]{0,1:T(8,128)(2,1)} fusion(bf16[1376,4096]{1,0:T(8,128)(2,1)} %param.22, bf16[4096,1376]{0,1:T(8,128)(2,1)} %param.21, f32[256,1376]{0,1:T(8,128)} %fusion.35, bf16[256,4096]{1,0:T(8,128)(2,1)} %all-gather.5.cloned.1.call-done, f32[4096]{0:T(1024)S(1)} %convert_element_type.91, f32[256]{0:T(256)S(1)} %add_rsqrt_fusion), kind=kOutput, calls=%fused_computation.18 | convolution fusion | flops 5778718720 | bytes 28165120 | tf_op jit(solution)/shard_map/dot_general | solution.py:36
  199.3 34.6 %reduce-scatter.5.cloned.1.call-done = bf16[512,256]{0,1:T(8,128)(2,1)} async-done(((bf16[4096,256]{0,1:T(8,128)(2,1)}), bf16[512,256]{0,1:T(8,128)(2,1)}) %reduce-scatter.5.cloned.1.call-update) | async-done | bytes 262160 | tf_op jit(solution)/shard_map/reduce_scatter | solution.py:139
  233.8 1.8 fusion.42
  (67 shorter events, 11.7 us)
Async XLA Ops:
  7.2 38.2 %copy-start = (bf16[4096,128]{1,0:T(8,128)(2,1)S(1)}, bf16[4096,128]{1,0:T(8,128)(2,1)}, u32[]{:S(2)}) copy-start(bf16[4096,128]{1,0:T(8,128)(2,1)} %param.18) | copy-start | bytes 3145732
  7.2 36.0 %all-gather.3.cloned.1.call-start = ((), (), s32[]{:S(2)}) async-start(), calls=%async_computation.2 | async-start | bytes 2359296 | tf_op jit(solution)/shard_map/all_gather | solution.py:87
  7.9 127.1 %reduce-scatter.3.cloned.1.call-start = ((), (), s32[]{:S(2)}) async-start(), calls=%async_computation.3 | async-start | bytes 2359296 | tf_op jit(solution)/shard_map/reduce_scatter | solution.py:130
  8.6 15.2 %collective-permute-start.2 = (s32[2,8]{1,0:T(2,128)S(1)}, s32[2,8]{1,0:T(2,128)S(1)}, u32[]{:S(2)}, u32[]{:S(2)}) collective-permute-start(s32[2,8]{1,0:T(2,128)S(1)} %pad_add_fusion.1), channel_id=1, source_target_pairs={{0,24},{8,0},{16,8},{24,16},{1,25},{9,1},{17,9},{25,17},{2,26},{10... | collective-permute-start | bytes 200 | tf_op jit(solution)/shard_map/ppermute | solution.py:45
  12.5 11.4 %collective-permute-start.1 = (s32[2,8]{1,0:T(2,128)S(1)}, s32[2,8]{1,0:T(2,128)S(1)}, u32[]{:S(2)}, u32[]{:S(2)}) collective-permute-start(s32[2,8]{1,0:T(2,128)S(1)} %pad_add_fusion.1), channel_id=1, source_target_pairs={{0,16},{8,24},{16,0},{24,8},{1,17},{9,25},{17,1},{25,9},{2,18},{10... | collective-permute-start | bytes 200 | tf_op jit(solution)/shard_map/ppermute | solution.py:45
  13.0 10.9 %collective-permute-start = (s32[2,8]{1,0:T(2,128)S(1)}, s32[2,8]{1,0:T(2,128)S(1)}, u32[]{:S(2)}, u32[]{:S(2)}) collective-permute-start(s32[2,8]{1,0:T(2,128)S(1)} %pad_add_fusion.1), channel_id=1, source_target_pairs={{0,8},{8,16},{16,24},{24,0},{1,9},{9,17},{17,25},{25,1},{2,10},{10... | collective-permute-start | bytes 200 | tf_op jit(solution)/shard_map/ppermute | solution.py:45
  14.8 15.8 %collective-permute-start.5 = (bf16[8,128,256]{2,1,0:T(8,128)(2,1)S(1)}, bf16[8,128,256]{2,1,0:T(8,128)(2,1)S(1)}, u32[]{:S(2)}, u32[]{:S(2)}) collective-permute-start(bf16[8,128,256]{2,1,0:T(8,128)(2,1)S(1)} %pad_maximum_fusion.1), channel_id=1, source_target_pairs={{0,24},{8,0},{16,8},{24,16},{1,25},{9,1},{17,9},{25,17},{2,26},{10... | collective-permute-start | bytes 1572872 | tf_op jit(solution)/shard_map/ppermute | solution.py:45
  17.2 23.8 %collective-permute-start.4 = (bf16[8,128,256]{2,1,0:T(8,128)(2,1)S(1)}, bf16[8,128,256]{2,1,0:T(8,128)(2,1)S(1)}, u32[]{:S(2)}, u32[]{:S(2)}) collective-permute-start(bf16[8,128,256]{2,1,0:T(8,128)(2,1)S(1)} %pad_maximum_fusion.1), channel_id=1, source_target_pairs={{0,16},{8,24},{16,0},{24,8},{1,17},{9,25},{17,1},{25,9},{2,18},{10... | collective-permute-start | bytes 1572872 | tf_op jit(solution)/shard_map/ppermute | solution.py:45
  23.9 17.1 %collective-permute-start.3 = (bf16[8,128,256]{2,1,0:T(8,128)(2,1)S(1)}, bf16[8,128,256]{2,1,0:T(8,128)(2,1)S(1)}, u32[]{:S(2)}, u32[]{:S(2)}) collective-permute-start(bf16[8,128,256]{2,1,0:T(8,128)(2,1)S(1)} %pad_maximum_fusion.1), channel_id=1, source_target_pairs={{0,8},{8,16},{16,24},{24,0},{1,9},{9,17},{17,25},{25,1},{2,10},{10... | collective-permute-start | bytes 1572872 | tf_op jit(solution)/shard_map/ppermute | solution.py:45
  43.1 19.2 %copy-start.4 = (bf16[256,4096]{1,0:T(8,128)(2,1)S(1)}, bf16[256,4096]{1,0:T(8,128)(2,1)}, u32[]{:S(2)}) copy-start(bf16[256,4096]{1,0:T(8,128)(2,1)} %all-gather.3.cloned.1.call-done) | copy-start | bytes 6291460
  43.1 19.2 %copy-start.8 = (bf16[4096,512]{1,0:T(8,128)(2,1)S(1)}, bf16[4096,512]{1,0:T(8,128)(2,1)}, u32[]{:S(2)}) copy-start(bf16[4096,512]{1,0:T(8,128)(2,1)} %param.17) | copy-start | bytes 12582916
  74.0 18.6 %copy-start.6 = (bf16[4096,128]{0,1:T(8,128)(2,1)S(1)}, bf16[4096,128]{0,1:T(8,128)(2,1)}, u32[]{:S(2)}) copy-start(bf16[4096,128]{0,1:T(8,128)(2,1)} %copy.25) | copy-start | bytes 3145732
  92.6 5.0 %copy-start.2 = (bf16[512,4096]{1,0:T(8,128)(2,1)S(1)}, bf16[512,4096]{1,0:T(8,128)(2,1)}, u32[]{:S(2)}) copy-start(bf16[512,4096]{1,0:T(8,128)(2,1)} %param.19) | copy-start | bytes 12582916
  97.6 37.4 %copy-start.5 = (bf16[256,512]{1,0:T(8,128)(2,1)S(1)}, bf16[256,512]{1,0:T(8,128)(2,1)}, u32[]{:S(2)}) copy-start(bf16[256,512]{1,0:T(8,128)(2,1)} %param.14) | copy-start | bytes 786436
  97.6 39.4 %copy-start.7 = (bf16[4096]{0:T(1024)(128)(2,1)S(1)}, bf16[4096]{0:T(1024)(128)(2,1)}, u32[]{:S(2)}) copy-start(bf16[4096]{0:T(1024)(128)(2,1)} %param.16) | copy-start | bytes 24580
  100.3 64.6 %all-gather.5.cloned.1.call-start = ((), (), s32[]{:S(2)}) async-start(), calls=%async_computation.4 | async-start | bytes 2359296 | tf_op jit(solution)/shard_map/all_gather | solution.py:134
  136.8 97.0 %reduce-scatter.5.cloned.1.call-start = ((), (), s32[]{:S(2)}) async-start(), calls=%async_computation.5 | async-start | bytes 2359296 | tf_op jit(solution)/shard_map/reduce_scatter | solution.py:139
  176.2 57.6 %copy-start.3 = (bf16[256,512]{1,0:T(8,128)(2,1)S(1)}, bf16[256,512]{1,0:T(8,128)(2,1)}, u32[]{:S(2)}) copy-start(bf16[256,512]{1,0:T(8,128)(2,1)} %fusion.41) | copy-start | bytes 786436
  176.2 59.4 %copy-start.1 = (bf16[4096,128]{1,0:T(8,128)(2,1)S(1)}, bf16[4096,128]{1,0:T(8,128)(2,1)}, u32[]{:S(2)}) copy-start(bf16[4096,128]{1,0:T(8,128)(2,1)} %param.18) | copy-start | bytes 3145732
Sparse Core Ops, SparseCore 0:
  9.6 31.7 all-gather.2
  100.4 34.5 reduce-scatter.2
  137.2 27.6 all-gather.4
  198.5 35.2 reduce-scatter.4
where the time goes:
time: 242 us
  waiting for transfers between devices  108 us (45%)
  matrix products  51.5 us (21%)
  other arithmetic  38 us (16%)
  blocking collectives  14.3 us (6%)
  between operations  14 us (6%)
  starting transfers between devices  9.33 us (4%)
  local copies, waits for them, and re-layouts  6.72 us (3%)
    reduce_scatter x1, waiting for transfers between devices, per_device(): lax.psum_scatter(column_term(attn_rows, w_out).astype(jnp.bfloat16), 'tp'...  34.6 us
    reduce_scatter x1, waiting for transfers between devices, per_device(): lax.psum_scatter(column_term(hidden, w_down).astype(jnp.bfloat16), 'tp',...  34.6 us
    all_gather x1, waiting for transfers between devices, per_device(): full_mid = lax.all_gather(mid, 'tp', axis=1, tiled=True)  27.9 us
    dot_general x2, matrix products, column_term(): lax.dot_general(weight, rows, (((0,), (1,)), ((), ())), preferred_element...  24.8 us
    sub x1, other arithmetic, per_device(): weights = jnp.where(valid[None], jnp.exp(scores - peak[..., None]), 0.0)  18.6 us
    all_gather x1, blocking collectives, per_device(): kv_all = lax.all_gather(kv_piece, 'tp', axis=1, tiled=True)  14.3 us
    ppermute x6, waiting for transfers between devices, gather_ctx(): parts.append(lax.ppermute(value, 'ctx', pairs))  10.4 us
    dot_general x1, matrix products, per_device(): gate = jnp.dot(x_two, w_gate, preferred_element_type=jnp.float32)  9.17 us
  transfers between devices with their start and end apart: 10, of which 4 were waited for; matrix products, arithmetic and copies ran while one was open for 7% of the time, Pallas kernels for 0%

commit v1 on v0

--- a/solution.py
+++ b/solution.py
@@ -10,6 +10,18 @@
 THETA = 5000000.0
 EPS = 1e-05
 NEG = -1e30
+
+
+def doubled_up(shard, axis, dim):
+    ways, here, step = (lax.axis_size(axis), lax.axis_index(axis), shard.shape[dim])
+    line, have = (shard, 1)
+    while have < ways:
+        line = jnp.concatenate(
+            [line, lax.ppermute(line, axis, [(d, (d - have) % ways) for d in range(ways)])],
+            axis=dim,
+        )
+        have = 2 * have
+    return jnp.roll(line, here * step, axis=dim)
 
 
 def rms_norm(values, gain):
@@ -131,7 +143,7 @@
         column_term(attn_rows, w_out).astype(jnp.bfloat16), "tp", scatter_dimension=0, tiled=True
     ).astype(jnp.float32)
     mid = (resid.astype(jnp.float32) + head_sum.T).astype(jnp.bfloat16)
-    full_mid = lax.all_gather(mid, "tp", axis=1, tiled=True)
+    full_mid = doubled_up(mid, "tp", 1)
     x_two = rms_norm(full_mid, mlp_gain)
     gate = jnp.dot(x_two, w_gate, preferred_element_type=jnp.float32)
     up_part = jnp.dot(x_two, w_up, preferred_element_type=jnp.float32)

time: 242 us -> 286 us (1.18)
  waiting for transfers between devices: 108 us -> 143 us
  local copies, waits for them, and re-layouts: 6.72 us -> 12.8 us
    ppermute x0 -> x3, waiting for transfers between devices: none -> 63.1 us  [doubled_up(): lax.ppermute(line, axis, [(d, (d - have) % ways) for d in range(ways)])]
    all_gather x1 -> x0, waiting for transfers between devices: 27.9 us -> none  [per_device(): full_mid = lax.all_gather(mid, 'tp', axis=1, tiled=True)]
    unnamed x18 -> x24, local copies, waits for them, and re-layouts: 0.05 us -> 5.12 us
  transfers between devices with their start and end apart: 10 -> 12, of which waited for: 4 -> 6; matrix products, arithmetic and copies ran while one was open for 7% -> 6% of each run, Pallas kernels for 0% -> 0%
where the time goes in v1:
time: 286 us
  waiting for transfers between devices  143 us (50%)
  matrix products  51.8 us (18%)
  other arithmetic  39.9 us (14%)
  blocking collectives  14.3 us (5%)
  between operations  14 us (5%)
  local copies, waits for them, and re-layouts  12.8 us (4%)
  starting transfers between devices  10.4 us (4%)
    ppermute x3, waiting for transfers between devices, doubled_up(): lax.ppermute(line, axis, [(d, (d - have) % ways) for d in range(ways)])  63.1 us
    reduce_scatter x1, waiting for transfers between devices, per_device(): lax.psum_scatter(column_term(attn_rows, w_out).astype(jnp.bfloat16), 'tp'...  34.7 us
    reduce_scatter x1, waiting for transfers between devices, per_device(): lax.psum_scatter(column_term(hidden, w_down).astype(jnp.bfloat16), 'tp',...  33.8 us
    dot_general x2, matrix products, column_term(): lax.dot_general(weight, rows, (((0,), (1,)), ((), ())), preferred_element...  25.1 us
    sub x1, other arithmetic, per_device(): weights = jnp.where(valid[None], jnp.exp(scores - peak[..., None]), 0.0)  18.6 us
    all_gather x1, blocking collectives, per_device(): kv_all = lax.all_gather(kv_piece, 'tp', axis=1, tiled=True)  14.3 us
    ppermute x6, waiting for transfers between devices, gather_ctx(): parts.append(lax.ppermute(value, 'ctx', pairs))  10.4 us
    dot_general x1, matrix products, per_device(): gate = jnp.dot(x_two, w_gate, preferred_element_type=jnp.float32)  9.14 us
  transfers between devices with their start and end apart: 12, of which 6 were waited for; matrix products, arithmetic and copies ran while one was open for 6% of the time, Pallas kernels for 0%

profile of v1, /device:TPU:0, one launch (start us, length us, event | category | flops | bytes accessed | tf_op | source)
XLA Modules:
  0.0 286.0 jit_solution(10277989123408768211)
XLA Ops:
  8.6 3.9 %collective-permute-start.2 = (s32[2,8]{1,0:T(2,128)S(1)}, s32[2,8]{1,0:T(2,128)S(1)}, u32[]{:S(2)}, u32[]{:S(2)}) collective-permute-start(s32[2,8]{1,0:T(2,128)S(1)} %pad_add_fusion.1), channel_id=1, source_target_pairs={{0,24},{8,0},{16,8},{24,16},{1,25},{9,1},{17,9},{25,17},{2,26},{10... | collective-permute-start | bytes 200 | tf_op jit(solution)/shard_map/ppermute | solution.py:57
  14.8 2.4 collective-permute-start.5
  17.2 1.5 collective-permute-start.4
  25.5 5.1 %pad_add_fusion = pred[256,4352]{0,1:T(8,128)(4,1)} fusion(pred[256,256]{0,1:T(8,128)(4,1)S(1)} %fusion.48, pred[4352]{0:T(1024)(128)(4,1)S(1)} %pad.13.clone), kind=kLoop, calls=%fused_computation.20 | loop fusion | flops 1114112 | bytes 1184000 | tf_op jit(solution)/shard_map/concatenate | solution.py:124
  30.6 10.4 %collective-permute-done.4 = bf16[8,128,256]{2,1,0:T(8,128)(2,1)S(1)} collective-permute-done((bf16[8,128,256]{2,1,0:T(8,128)(2,1)S(1)}, bf16[8,128,256]{2,1,0:T(8,128)(2,1)S(1)}, u32[]{:S(2)}, u32[]{:S(2)}) %collective-permute-start.4) | collective-permute-done | bytes 524320 | tf_op jit(solution)/shard_map/ppermute | solution.py:57
  41.8 1.3 copy.25
  43.1 2.2 fusion.12
  45.4 2.6 convolution_convert_fusion.2
  48.0 14.3 %all_gather.7 = bf16[256,1024]{1,0:T(8,128)(2,1)S(1)} all-gather(bf16[256,128]{1,0:T(8,128)(2,1)S(1)} %convolution_convert_fusion.2), channel_id=1, replica_groups=mesh['ctx'=4,'tp'=8] {'tp'}, dimensions={1}, use_global_device_ids=true | all-gather | bytes 589824 | tf_op jit(solution)/shard_map/all_gather | solution.py:109
  63.0 1.3 fusion.35
  66.0 8.7 %fusion.29 = f32[4352,256,4]{1,0,2:T(8,128)} fusion(bf16[256,128]{1,0:T(8,128)(2,1)S(1)} %dynamic-slice_bitcast_fusion, bf16[4096,128]{1,0:T(8,128)(2,1)S(1)} %bitcast.70, bf16[256,4,64]{2,0,1:T(8,128)(2,1)S(1)} %get-tuple-element.9, bf16[256,4,64]{2,0,1:T(8,128)(2,1)S(1)} %get-tuple-element.8), kind=kOutput, calls=%fused_computation.37 | convolution fusion | flops 1143603200 | bytes 19202048 | tf_op jit(solution)/shard_map/chd,kd->hck/dot_general | solution.py:127
  74.6 18.6 %fusion.66 = (f32[4,256]{1,0:T(4,128)S(1)}, bf16[4,256,4352]{1,2,0:T(8,128)(2,1)}) fusion(f32[4352,256,4]{1,0,2:T(8,128)} %fusion.29, pred[256,4352]{0,1:T(8,128)(4,1)} %pad_add_fusion), kind=kOutput, calls=%fused_computation.105 | output fusion | flops 31199488 | bytes 27856896 | tf_op jit(solution)/shard_map/sub | solution.py:131
  93.3 5.0 %fusion.24 = bf16[256,4,128]{0,2,1:T(8,128)(2,1)S(1)} fusion(bf16[4,256,4352]{1,2,0:T(8,128)(2,1)} %get-tuple-element.21, bf16[256,128]{0,1:T(8,128)(2,1)S(1)} %copy.21, bf16[4096,128]{0,1:T(8,128)(2,1)S(1)} %copy-done.5, f32[256,4]{0,1:T(4,128)S(1)} %bitcast.77), kind=kOutput, calls=%fused_computation.31 | convolution fusion | flops 1143341056 | bytes 10293248 | tf_op jit(solution)/shard_map/hck,kd->hcd/dot_general | solution.py:133
  98.3 2.7 fusion.11
  101.0 34.7 %reduce-scatter.3.cloned.1.call-done = bf16[512,256]{0,1:T(8,128)(2,1)} async-done(((bf16[4096,256]{0,1:T(8,128)(2,1)}), bf16[512,256]{0,1:T(8,128)(2,1)}) %reduce-scatter.3.cloned.1.call-update) | async-done | bytes 262160 | tf_op jit(solution)/shard_map/reduce_scatter | solution.py:142
  135.7 1.8 constant_dynamic-update-slice_fusion.7
  138.5 3.9 %collective-permute-done.6 = bf16[256,512]{1,0:T(8,128)(2,1)S(1)} collective-permute-done((bf16[256,512]{1,0:T(8,128)(2,1)S(1)}, bf16[256,512]{1,0:T(8,128)(2,1)S(1)}, u32[]{:S(2)}, u32[]{:S(2)}) %collective-permute-start.6) | collective-permute-done | bytes 262176 | tf_op jit(solution)/shard_map/ppermute | solution.py:20
  142.8 11.7 %collective-permute-done.7 = bf16[256,1024]{1,0:T(8,128)(2,1)S(1)} collective-permute-done((bf16[256,1024]{1,0:T(8,128)(2,1)S(1)}, bf16[256,1024]{1,0:T(8,128)(2,1)S(1)}, u32[]{:S(2)}, u32[]{:S(2)}) %collective-permute-start.7) | collective-permute-done | bytes 524320 | tf_op jit(solution)/shard_map/ppermute | solution.py:20
  157.2 47.5 %collective-permute-done.8 = bf16[256,2048]{1,0:T(8,128)(2,1)S(1)} collective-permute-done((bf16[256,2048]{1,0:T(8,128)(2,1)}, bf16[256,2048]{1,0:T(8,128)(2,1)S(1)}, u32[]{:S(2)}, u32[]{:S(2)}) %collective-permute-start.8) | collective-permute-done | bytes 1048608 | tf_op jit(solution)/shard_map/ppermute | solution.py:20
  209.3 2.1 fusion.15
  211.3 9.1 %fusion.42 = f32[256,1376]{0,1:T(8,128)} fusion(bf16[4096,1376]{0,1:T(8,128)(2,1)} %param.20, f32[4096]{0:T(1024)S(1)} %convert_element_type.91, f32[256]{0:T(256)S(1)} %add_rsqrt_fusion, bf16[256,8192]{1,0:T(8,128)(2,1)} %constant_dynamic-update-slice_fusion, s32[]{:T(128)S(6)} %select_n.58), kind=kOutput, calls=%fused_computation.57 | convolution fusion | flops 2889875456 | bytes 14795780 | tf_op jit(solution)/shard_map/dot_general | solution.py:148
  220.5 22.4 %fusion.10 = bf16[4096,256]{0,1:T(8,128)(2,1)} fusion(bf16[1376,4096]{1,0:T(8,128)(2,1)} %param.22, f32[256,1376]{0,1:T(8,128)} %fusion.42, bf16[4096,1376]{0,1:T(8,128)(2,1)} %param.21, f32[4096]{0:T(1024)S(1)} %convert_element_type.91, f32[256]{0:T(256)S(1)} %add_rsqrt_fusion, bf16[256,8192]{1,0:T(8,128)(2,1)} %constant_dynamic-update-slice_fusion, ...), kind=kOutput, calls=%fused_computation.18 | convolution fusion | flops 5778718720 | bytes 28165124 | tf_op jit(solution)/shard_map/dot_general | solution.py:48
  243.8 33.8 %reduce-scatter.5.cloned.1.call-done = bf16[512,256]{0,1:T(8,128)(2,1)} async-done(((bf16[4096,256]{0,1:T(8,128)(2,1)}), bf16[512,256]{0,1:T(8,128)(2,1)}) %reduce-scatter.5.cloned.1.call-update) | async-done | bytes 262160 | tf_op jit(solution)/shard_map/reduce_scatter | solution.py:151
  277.7 1.8 fusion.44
  (79 shorter events, 23.2 us)
Async XLA Ops:
  7.2 38.2 %copy-start = (bf16[4096,128]{1,0:T(8,128)(2,1)S(1)}, bf16[4096,128]{1,0:T(8,128)(2,1)}, u32[]{:S(2)}) copy-start(bf16[4096,128]{1,0:T(8,128)(2,1)} %param.18) | copy-start | bytes 3145732
  7.2 35.9 %all-gather.2.cloned.1.call-start = ((), (), s32[]{:S(2)}) async-start(), calls=%async_computation.2 | async-start | bytes 2359296 | tf_op jit(solution)/shard_map/all_gather | solution.py:99
  7.9 127.8 %reduce-scatter.3.cloned.1.call-start = ((), (), s32[]{:S(2)}) async-start(), calls=%async_computation.3 | async-start | bytes 2359296 | tf_op jit(solution)/shard_map/reduce_scatter | solution.py:142
  8.6 15.2 %collective-permute-start.2 = (s32[2,8]{1,0:T(2,128)S(1)}, s32[2,8]{1,0:T(2,128)S(1)}, u32[]{:S(2)}, u32[]{:S(2)}) collective-permute-start(s32[2,8]{1,0:T(2,128)S(1)} %pad_add_fusion.1), channel_id=1, source_target_pairs={{0,24},{8,0},{16,8},{24,16},{1,25},{9,1},{17,9},{25,17},{2,26},{10... | collective-permute-start | bytes 200 | tf_op jit(solution)/shard_map/ppermute | solution.py:57
  12.5 11.4 %collective-permute-start.1 = (s32[2,8]{1,0:T(2,128)S(1)}, s32[2,8]{1,0:T(2,128)S(1)}, u32[]{:S(2)}, u32[]{:S(2)}) collective-permute-start(s32[2,8]{1,0:T(2,128)S(1)} %pad_add_fusion.1), channel_id=1, source_target_pairs={{0,16},{8,24},{16,0},{24,8},{1,17},{9,25},{17,1},{25,9},{2,18},{10... | collective-permute-start | bytes 200 | tf_op jit(solution)/shard_map/ppermute | solution.py:57
  13.0 10.9 %collective-permute-start = (s32[2,8]{1,0:T(2,128)S(1)}, s32[2,8]{1,0:T(2,128)S(1)}, u32[]{:S(2)}, u32[]{:S(2)}) collective-permute-start(s32[2,8]{1,0:T(2,128)S(1)} %pad_add_fusion.1), channel_id=1, source_target_pairs={{0,8},{8,16},{16,24},{24,0},{1,9},{9,17},{17,25},{25,1},{2,10},{10... | collective-permute-start | bytes 200 | tf_op jit(solution)/shard_map/ppermute | solution.py:57
  14.8 15.8 %collective-permute-start.5 = (bf16[8,128,256]{2,1,0:T(8,128)(2,1)S(1)}, bf16[8,128,256]{2,1,0:T(8,128)(2,1)S(1)}, u32[]{:S(2)}, u32[]{:S(2)}) collective-permute-start(bf16[8,128,256]{2,1,0:T(8,128)(2,1)S(1)} %pad_maximum_fusion.2), channel_id=1, source_target_pairs={{0,24},{8,0},{16,8},{24,16},{1,25},{9,1},{17,9},{25,17},{2,26},{10... | collective-permute-start | bytes 1572872 | tf_op jit(solution)/shard_map/ppermute | solution.py:57
  17.2 23.8 %collective-permute-start.4 = (bf16[8,128,256]{2,1,0:T(8,128)(2,1)S(1)}, bf16[8,128,256]{2,1,0:T(8,128)(2,1)S(1)}, u32[]{:S(2)}, u32[]{:S(2)}) collective-permute-start(bf16[8,128,256]{2,1,0:T(8,128)(2,1)S(1)} %pad_maximum_fusion.2), channel_id=1, source_target_pairs={{0,16},{8,24},{16,0},{24,8},{1,17},{9,25},{17,1},{25,9},{2,18},{10... | collective-permute-start | bytes 1572872 | tf_op jit(solution)/shard_map/ppermute | solution.py:57
  23.9 17.1 %collective-permute-start.3 = (bf16[8,128,256]{2,1,0:T(8,128)(2,1)S(1)}, bf16[8,128,256]{2,1,0:T(8,128)(2,1)S(1)}, u32[]{:S(2)}, u32[]{:S(2)}) collective-permute-start(bf16[8,128,256]{2,1,0:T(8,128)(2,1)S(1)} %pad_maximum_fusion.2), channel_id=1, source_target_pairs={{0,8},{8,16},{16,24},{24,0},{1,9},{9,17},{17,25},{25,1},{2,10},{10... | collective-permute-start | bytes 1572872 | tf_op jit(solution)/shard_map/ppermute | solution.py:57
  43.1 19.9 %copy-start.3 = (bf16[256,4096]{1,0:T(8,128)(2,1)S(1)}, bf16[256,4096]{1,0:T(8,128)(2,1)}, u32[]{:S(2)}) copy-start(bf16[256,4096]{1,0:T(8,128)(2,1)} %all-gather.2.cloned.1.call-done) | copy-start | bytes 6291460
  43.1 19.9 %copy-start.8 = (bf16[4096,512]{1,0:T(8,128)(2,1)S(1)}, bf16[4096,512]{1,0:T(8,128)(2,1)}, u32[]{:S(2)}) copy-start(bf16[4096,512]{1,0:T(8,128)(2,1)} %param.17) | copy-start | bytes 12582916
  74.6 18.6 %copy-start.5 = (bf16[4096,128]{0,1:T(8,128)(2,1)S(1)}, bf16[4096,128]{0,1:T(8,128)(2,1)}, u32[]{:S(2)}) copy-start(bf16[4096,128]{0,1:T(8,128)(2,1)} %copy.25) | copy-start | bytes 3145732
  93.2 5.0 %copy-start.2 = (bf16[512,4096]{1,0:T(8,128)(2,1)S(1)}, bf16[512,4096]{1,0:T(8,128)(2,1)}, u32[]{:S(2)}) copy-start(bf16[512,4096]{1,0:T(8,128)(2,1)} %param.19) | copy-start | bytes 12582916
  98.3 37.4 %copy-start.6 = (bf16[256,512]{1,0:T(8,128)(2,1)S(1)}, bf16[256,512]{1,0:T(8,128)(2,1)}, u32[]{:S(2)}) copy-start(bf16[256,512]{1,0:T(8,128)(2,1)} %param.14) | copy-start | bytes 786436
  100.9 54.7 %copy-start.7 = (bf16[4096]{0:T(1024)(128)(2,1)S(1)}, bf16[4096]{0:T(1024)(128)(2,1)}, u32[]{:S(2)}) copy-start(bf16[4096]{0:T(1024)(128)(2,1)} %param.16) | copy-start | bytes 24580
  101.0 176.7 %reduce-scatter.5.cloned.1.call-start = ((), (), s32[]{:S(2)}) async-start(), calls=%async_computation.4 | async-start | bytes 2359296 | tf_op jit(solution)/shard_map/reduce_scatter | solution.py:151
  137.5 5.0 %collective-permute-start.6 = (bf16[256,512]{1,0:T(8,128)(2,1)S(1)}, bf16[256,512]{1,0:T(8,128)(2,1)S(1)}, u32[]{:S(2)}, u32[]{:S(2)}) collective-permute-start(bf16[256,512]{1,0:T(8,128)(2,1)S(1)} %get-tuple-element.3), channel_id=1, source_target_pairs={{0,7},{1,0},{2,1},{3,2},{4,3},{5,4},{6,5},{7,6},{8,15},{9,8},{10,9... | collective-permute-start | bytes 786440 | tf_op jit(solution)/shard_map/ppermute | solution.py:20
  142.5 12.0 %collective-permute-start.7 = (bf16[256,1024]{1,0:T(8,128)(2,1)S(1)}, bf16[256,1024]{1,0:T(8,128)(2,1)S(1)}, u32[]{:S(2)}, u32[]{:S(2)}) collective-permute-start(bf16[256,1024]{1,0:T(8,128)(2,1)S(1)} %pad_maximum_fusion.3), channel_id=1, source_target_pairs={{0,6},{1,7},{2,0},{3,1},{4,2},{5,3},{6,4},{7,5},{8,14},{9,15},{10,... | collective-permute-start | bytes 1572872 | tf_op jit(solution)/shard_map/ppermute | solution.py:20
  155.6 49.1 %collective-permute-start.8 = (bf16[256,2048]{1,0:T(8,128)(2,1)}, bf16[256,2048]{1,0:T(8,128)(2,1)S(1)}, u32[]{:S(2)}, u32[]{:S(2)}) collective-permute-start(bf16[256,2048]{1,0:T(8,128)(2,1)} %pad_maximum_fusion.1), channel_id=1, source_target_pairs={{0,4},{1,5},{2,6},{3,7},{4,0},{5,1},{6,2},{7,3},{8,12},{9,13},{10,... | collective-permute-start | bytes 3145736 | tf_op jit(solution)/shard_map/ppermute | solution.py:20
  220.5 22.6 %copy-start.4 = (bf16[256,512]{1,0:T(8,128)(2,1)S(1)}, bf16[256,512]{1,0:T(8,128)(2,1)}, u32[]{:S(2)}) copy-start(bf16[256,512]{1,0:T(8,128)(2,1)} %get-tuple-element.12) | copy-start | bytes 786436
  220.5 58.9 %copy-start.1 = (bf16[4096,128]{1,0:T(8,128)(2,1)S(1)}, bf16[4096,128]{1,0:T(8,128)(2,1)}, u32[]{:S(2)}) copy-start(bf16[4096,128]{1,0:T(8,128)(2,1)} %param.18) | copy-start | bytes 3145732
Sparse Core Ops, SparseCore 0:
  9.6 31.7 all-gather.1
  101.1 34.5 reduce-scatter.2
  243.0 34.5 reduce-scatter.4
